TPU v7x, 512 devices: a whole 4x4x16 slice. The times are simulated.
512 devices in a mesh: exp: 32 (over z, core), rep: 16 (over y, x).
Axes of the slice: x: 4, y: 4, z: 16, core: 2. Of those that a mesh axis runs over, the one named last changes fastest.
Arguments:
- tokens: bfloat16 [65536, 1536], P(('exp', 'rep')), may hold values from -6 to 6
- grad_out: bfloat16 [65536, 1536], P(('exp', 'rep')), may hold values from -6 to 6
- expert_ids: int32 [65536, 2], P(('exp', 'rep')), may hold values from 0 to 31, all different within a row; in each aligned block of 128 rows (0 to 127, 128 to 255, ...) at most 10 rows name the same one
- probs: bfloat16 [65536, 2], P(('exp', 'rep')), may hold values from 0.099609375 to 1
- w_gate: bfloat16 [32, 768, 1536], P('exp', 'rep'), may hold values from -0.15625 to 0.15625
- w_up: bfloat16 [32, 768, 1536], P('exp', 'rep'), may hold values from -0.15625 to 0.15625
- w_down: bfloat16 [32, 768, 1536], P('exp', 'rep'), may hold values from -0.21875 to 0.21875
Outputs:
- grad_tokens: bfloat16 [65536, 1536], P(('exp', 'rep'))
- grad_probs: float32 [65536, 2], P(('exp', 'rep'))
- grad_gate: float32 [32, 768, 1536], P('exp', 'rep')
- grad_up: float32 [32, 768, 1536], P('exp', 'rep')
- grad_down: float32 [32, 768, 1536], P('exp', 'rep')
Inputs may be any that keep to these rules, and one draw needn't show every extreme that they name: `expert_ids`: each token names two different experts; among the 128 tokens of one device no expert is named more than 10 times, a bound that some block reaches.
All inputs are finite; a program needn't handle non-finite values.
Results may differ from a plain program's by a relative error of at most 0.007.
Values may be sent and summed in bfloat16 or wider, within the bound.
No kernel may reach another device: no remote copies, remote signals or barrier semaphores. Data moves between devices by JAX's collectives and lax.ppermute only.
A program may use at most 64 MiB of HBM per device.

v0:
```python
import jax
import jax.numpy as jnp
from jax import lax
from jax.sharding import Mesh
from jax.sharding import PartitionSpec as P

LANE = 128


def swap_pair(value):
    return lax.ppermute(value, "rl", [(0, 1), (1, 0)])


def exchange(blocks):
    shape = blocks.shape
    split = blocks.reshape((lax.axis_size("ez"), lax.axis_size("ec")) + shape[1:])
    split = lax.all_to_all(split, "ez", split_axis=0, concat_axis=0, tiled=True)
    split = lax.all_to_all(split, "ec", split_axis=1, concat_axis=1, tiled=True)
    return split.reshape(shape)


def shards(tokens, grad_out, expert_ids, probs, w_gate, w_up, w_down):
    token_count = tokens.shape[0]
    width = tokens.shape[1]
    exp_count = lax.axis_size("ez") * lax.axis_size("ec")
    capacity = 5 * token_count // (2 * exp_count)
    slots = exp_count * capacity
    chosen = expert_ids.reshape(-1)
    onehot = (chosen[:, None] == jnp.arange(exp_count, dtype=jnp.int32)[None, :]).astype(jnp.int32)
    ranks = jnp.sum((jnp.cumsum(onehot, axis=0) - 1) * onehot, axis=1)
    slot_of = chosen * capacity + ranks
    routing = (slot_of[None, :] == jnp.arange(slots, dtype=jnp.int32)[:, None]).astype(jnp.bfloat16)
    token_routing = routing.reshape(slots, token_count, 2).sum(axis=2)
    prob_pairs = probs.reshape(-1, 1)
    slot_tokens = jnp.dot(token_routing, tokens, preferred_element_type=jnp.float32).astype(
        jnp.bfloat16
    )
    slot_grads = jnp.dot(token_routing, grad_out, preferred_element_type=jnp.float32).astype(
        jnp.bfloat16
    )
    slot_probs = jnp.dot(routing, prob_pairs, preferred_element_type=jnp.float32).astype(
        jnp.bfloat16
    )
    prob_block = jnp.concatenate([slot_probs, jnp.zeros((slots, LANE - 1), jnp.bfloat16)], axis=1)
    send_t = jnp.concatenate([slot_tokens, prob_block], axis=1).reshape(exp_count, capacity, -1)
    arrived_t = exchange(send_t).reshape(slots, -1)
    send_g = slot_grads.reshape(exp_count, capacity, -1)
    arrived_g = exchange(send_g).reshape(slots, -1)
    stacked = jnp.concatenate([w_gate, w_up, w_down], axis=0)
    full = lax.all_gather(stacked, "rh", axis=1, tiled=True)
    gate_w = full[0]
    up_w = full[1]
    down_w = full[2]

    def block(arrived_rows, grads):
        rows = arrived_rows[:, :width]
        weight = arrived_rows[:, width : width + 1].astype(jnp.float32)
        gate = jnp.dot(rows, gate_w.T, preferred_element_type=jnp.float32)
        up = jnp.dot(rows, up_w.T, preferred_element_type=jnp.float32)
        sig = jax.nn.sigmoid(gate)
        act = gate * sig
        hidden = act * up
        back = jnp.dot(grads, down_w.T, preferred_element_type=jnp.float32)
        prob_part = jnp.sum(hidden * back, axis=1, keepdims=True)
        d_gate = (weight * back * up * sig * (1.0 + gate * (1.0 - sig))).astype(jnp.bfloat16)
        d_up = (weight * back * act).astype(jnp.bfloat16)
        weighted = (weight * hidden).astype(jnp.bfloat16)
        partial_rows = jnp.dot(d_gate, gate_w, preferred_element_type=jnp.float32) + jnp.dot(
            d_up, up_w, preferred_element_type=jnp.float32
        )
        packed = jnp.concatenate(
            [
                partial_rows.astype(jnp.bfloat16),
                prob_part.astype(jnp.bfloat16),
                jnp.zeros((rows.shape[0], LANE - 1), jnp.bfloat16),
            ],
            axis=1,
        )
        local = jnp.stack(
            [
                jnp.dot(d_gate.T, rows, preferred_element_type=jnp.float32),
                jnp.dot(d_up.T, rows, preferred_element_type=jnp.float32),
                jnp.dot(weighted.T, grads, preferred_element_type=jnp.float32),
            ]
        )
        return (packed, local)

    partner_t = swap_pair(arrived_t)
    partner_g = swap_pair(arrived_g)
    packed_own, local_own = block(arrived_t, arrived_g)
    packed_partner, local_partner = block(partner_t, partner_g)
    received = swap_pair(packed_partner)
    weight_grads = lax.psum_scatter(
        (local_own + local_partner).astype(jnp.bfloat16), "rh", scatter_dimension=1, tiled=True
    ).astype(jnp.float32)
    summed = (packed_own.astype(jnp.float32) + received.astype(jnp.float32)).astype(jnp.bfloat16)
    returned = exchange(summed.reshape(exp_count, capacity, -1)).reshape(slots, -1)
    grad_tokens = jnp.dot(
        token_routing.T, returned[:, :width], preferred_element_type=jnp.float32
    ).astype(jnp.bfloat16)
    grad_probs = jnp.dot(
        routing.T, returned[:, width : width + 1], preferred_element_type=jnp.float32
    ).reshape(token_count, 2)
    return (grad_tokens, grad_probs, weight_grads[0:1], weight_grads[1:2], weight_grads[2:3])


def solution(mesh):
    exp_count = mesh.shape["exp"]
    rep_count = mesh.shape["rep"]
    view = Mesh(
        mesh.devices.reshape(exp_count // 2, 2, rep_count // 2, 2), ("ez", "ec", "rh", "rl")
    )
    rows_spec = P(("ez", "ec", "rh", "rl"), None)
    weight_spec = P(("ez", "ec"), ("rh", "rl"), None)
    in_specs = (rows_spec,) * 4 + (weight_spec,) * 3
    out_specs = (rows_spec, rows_spec, weight_spec, weight_spec, weight_spec)
    return jax.shard_map(shards, mesh=view, in_specs=in_specs, out_specs=out_specs, check_vma=False)
```

profile of v0, /device:TPU:1, one launch (start us, length us, event | category | flops | bytes accessed | tf_op | source)
XLA Modules:
  0.0 312.6 jit_solution(7887945041732350293)
XLA Ops:
  13.1 1.9 concatenate.22
  15.0 1.8 copy.69
  16.8 15.9 %all-to-all-start = ((bf16[16,2,10,1664]{3,1,2,0:T(2,128)(2,1)}), bf16[16,2,10,1664]{3,1,2,0:T(2,128)(2,1)S(1)}, u32[]{:S(2)}, u32[]{:S(2)}) async-start(bf16[16,2,10,1664]{3,1,2,0:T(2,128)(2,1)} %copy.69), calls=%async_computation | async-start | bytes 2129920 | tf_op jit(solution)/shard_map/all_to_all | solution.py:17
  35.0 1.4 reshape_reshape.17
  36.4 2.0 copy.72
  38.4 40.0 %all-to-all-done = bf16[16,2,10,1664]{3,1,2,0:T(2,128)(2,1)S(1)} async-done(((bf16[16,2,10,1664]{3,1,2,0:T(2,128)(2,1)}), bf16[16,2,10,1664]{3,1,2,0:T(2,128)(2,1)S(1)}, u32[]{:S(2)}, u32[]{:S(2)}) %all-to-all-start) | async-done | bytes 1064992 | tf_op jit(solution)/shard_map/all_to_all | solution.py:17
  78.4 10.1 %all_to_all.30 = bf16[16,2,10,1664]{3,0,2,1:T(8,128)(2,1)S(1)} all-to-all(bf16[16,2,10,1664]{3,0,2,1:T(8,128)(2,1)S(1)} %copy.70), channel_id=1, replica_groups=mesh['ez'=16,'ec'=2,'rh'=8,'rl'=2] {'ec'}, dimensions={1} | all-to-all | bytes 2129920 | tf_op jit(solution)/shard_map/all_to_all | solution.py:18
  88.5 7.7 %all-to-all-start.2 = ((bf16[16,2,10,1536]{3,1,2,0:T(2,128)(2,1)}), bf16[16,2,10,1536]{3,1,2,0:T(2,128)(2,1)}, u32[]{:S(2)}, u32[]{:S(2)}) async-start(bf16[16,2,10,1536]{3,1,2,0:T(2,128)(2,1)} %copy.72), calls=%async_computation.2 | async-start | bytes 1966080 | tf_op jit(solution)/shard_map/all_to_all | solution.py:17
  97.0 3.1 %collective-permute-start = (bf16[320,1664]{1,0:T(8,128)(2,1)S(1)}, bf16[320,1664]{1,0:T(8,128)(2,1)}, u32[]{:S(2)}, u32[]{:S(2)}) collective-permute-start(bf16[320,1664]{1,0:T(8,128)(2,1)S(1)} %reshape_reshape.16), channel_id=1, source_target_pairs={{0,1},{1,0},{2,3},{3,2},{4,5},{5,4},{6,7},{7,6},{8,9},{9,8},{10,11... | collective-permute-start | bytes 3194888 | tf_op jit(solution)/shard_map/ppermute | solution.py:11
  100.1 39.4 %all-to-all-done.2 = bf16[16,2,10,1536]{3,1,2,0:T(2,128)(2,1)} async-done(((bf16[16,2,10,1536]{3,1,2,0:T(2,128)(2,1)}), bf16[16,2,10,1536]{3,1,2,0:T(2,128)(2,1)}, u32[]{:S(2)}, u32[]{:S(2)}) %all-to-all-start.2) | async-done | bytes 983072 | tf_op jit(solution)/shard_map/all_to_all | solution.py:17
  139.5 1.4 copy.73
  140.9 9.5 %all_to_all.31 = bf16[16,2,10,1536]{3,0,2,1:T(8,128)(2,1)S(1)} all-to-all(bf16[16,2,10,1536]{3,0,2,1:T(8,128)(2,1)S(1)} %copy.73), channel_id=1, replica_groups=mesh['ez'=16,'ec'=2,'rh'=8,'rl'=2] {'ec'}, dimensions={1} | all-to-all | bytes 1966080 | tf_op jit(solution)/shard_map/all_to_all | solution.py:18
  152.1 3.3 %collective-permute-start.1 = (bf16[320,1536]{1,0:T(8,128)(2,1)}, bf16[320,1536]{1,0:T(8,128)(2,1)S(1)}, u32[]{:S(2)}, u32[]{:S(2)}) collective-permute-start(bf16[320,1536]{1,0:T(8,128)(2,1)} %reshape_reshape.18), channel_id=1, source_target_pairs={{0,1},{1,0},{2,3},{3,2},{4,5},{5,4},{6,7},{7,6},{8,9},{9,8},{10,11... | collective-permute-start | bytes 2949128 | tf_op jit(solution)/shard_map/ppermute | solution.py:11
  156.6 2.1 fusion.11
  163.6 1.9 fusion.9
  165.5 1.9 fusion.6
  167.4 9.7 %collective-permute-done.1 = bf16[320,1536]{1,0:T(8,128)(2,1)S(1)} collective-permute-done((bf16[320,1536]{1,0:T(8,128)(2,1)}, bf16[320,1536]{1,0:T(8,128)(2,1)S(1)}, u32[]{:S(2)}, u32[]{:S(2)}) %collective-permute-start.1) | collective-permute-done | bytes 983072 | tf_op jit(solution)/shard_map/ppermute | solution.py:11
  179.0 2.0 convolution_bitcast_fusion.1
  181.1 2.0 convolution_bitcast_fusion.2
  183.1 2.3 fusion
  187.4 1.6 fusion.8
  189.1 1.7 fusion.2
  191.4 3.1 concatenate.25
  194.5 3.2 %collective-permute-start.2 = (bf16[320,1664]{1,0:T(8,128)(2,1)}, bf16[320,1664]{1,0:T(8,128)(2,1)}, u32[]{:S(2)}, u32[]{:S(2)}) collective-permute-start(bf16[320,1664]{1,0:T(8,128)(2,1)} %concatenate.25), channel_id=1, source_target_pairs={{0,1},{1,0},{2,3},{3,2},{4,5},{5,4},{6,7},{7,6},{8,9},{9,8},{10,11... | collective-permute-start | bytes 3194888 | tf_op jit(solution)/shard_map/ppermute | solution.py:11
  198.5 1.6 fusion.10
  200.1 1.7 fusion.1
  201.8 2.3 concatenate.24
  204.1 25.7 %collective-permute-done.2 = bf16[320,1664]{1,0:T(8,128)(2,1)} collective-permute-done((bf16[320,1664]{1,0:T(8,128)(2,1)}, bf16[320,1664]{1,0:T(8,128)(2,1)}, u32[]{:S(2)}, u32[]{:S(2)}) %collective-permute-start.2) | collective-permute-done | bytes 1064992 | tf_op jit(solution)/shard_map/ppermute | solution.py:11
  229.8 1.5 add_convert_fusion
  232.6 60.0 %all_to_all.32 = bf16[16,2,10,1664]{3,1,2,0:T(2,128)(2,1)S(1)} all-to-all(bf16[16,2,10,1664]{3,1,2,0:T(2,128)(2,1)S(1)} %copy.77), channel_id=1, replica_groups=mesh['ez'=16,'ec'=2,'rh'=8,'rl'=2] {'ez'}, dimensions={0} | all-to-all | bytes 2129920 | tf_op jit(solution)/shard_map/all_to_all | solution.py:17
  292.7 8.3 %all_to_all.33 = bf16[16,2,10,1664]{3,0,2,1:T(8,128)(2,1)S(1)} all-to-all(bf16[16,2,10,1664]{3,0,2,1:T(8,128)(2,1)S(1)} %copy.78), channel_id=1, replica_groups=mesh['ez'=16,'ec'=2,'rh'=8,'rl'=2] {'ec'}, dimensions={1} | all-to-all | bytes 2129920 | tf_op jit(solution)/shard_map/all_to_all | solution.py:18
  303.7 2.0 fusion.39
  (90 shorter events, 25.9 us)
Async XLA Ops:
  7.2 4.4 %copy-start = (bf16[128,1536]{1,0:T(8,128)(2,1)S(1)}, bf16[128,1536]{1,0:T(8,128)(2,1)}, u32[]{:S(2)}) copy-start(bf16[128,1536]{1,0:T(8,128)(2,1)} %param.7) | copy-start | bytes 1179652
  11.1 22.5 %copy-start.5 = (bf16[320,128]{1,0:T(8,128)(2,1)}, bf16[320,128]{1,0:T(8,128)(2,1)S(1)}, u32[]{:S(2)}) copy-start(bf16[320,128]{1,0:T(8,128)(2,1)S(1)} %fusion.31) | copy-start | bytes 245764
  15.0 17.7 %copy-start.14 = (bf16[1,48,1536]{2,1,0:T(8,128)(2,1)S(1)}, bf16[1,48,1536]{2,1,0:T(8,128)(2,1)}, u32[]{:S(2)}) copy-start(bf16[1,48,1536]{2,1,0:T(8,128)(2,1)} %param.13) | copy-start | bytes 442372
  15.0 17.7 %copy-start.15 = (bf16[1,48,1536]{2,1,0:T(8,128)(2,1)S(1)}, bf16[1,48,1536]{2,1,0:T(8,128)(2,1)}, u32[]{:S(2)}) copy-start(bf16[1,48,1536]{2,1,0:T(8,128)(2,1)} %param.12) | copy-start | bytes 442372
  16.8 15.9 %copy-start.16 = (bf16[1,48,1536]{2,1,0:T(8,128)(2,1)S(1)}, bf16[1,48,1536]{2,1,0:T(8,128)(2,1)}, u32[]{:S(2)}) copy-start(bf16[1,48,1536]{2,1,0:T(8,128)(2,1)} %param.11) | copy-start | bytes 442372
  16.8 16.8 %copy-start.13 = (bf16[128,1536]{1,0:T(8,128)(2,1)S(1)}, bf16[128,1536]{1,0:T(8,128)(2,1)}, u32[]{:S(2)}) copy-start(bf16[128,1536]{1,0:T(8,128)(2,1)} %param.8) | copy-start | bytes 1179652
  16.8 61.5 %all-to-all-start = ((bf16[16,2,10,1664]{3,1,2,0:T(2,128)(2,1)}), bf16[16,2,10,1664]{3,1,2,0:T(2,128)(2,1)S(1)}, u32[]{:S(2)}, u32[]{:S(2)}) async-start(bf16[16,2,10,1664]{3,1,2,0:T(2,128)(2,1)} %copy.69), calls=%async_computation | async-start | bytes 2129920 | tf_op jit(solution)/shard_map/all_to_all | solution.py:17
  32.7 123.9 %all-gather.2.cloned.1.call-start = ((), (), s32[]{:S(2)}) async-start(), calls=%async_computation.7 | async-start | bytes 3981312 | tf_op jit(solution)/shard_map/all_gather | solution.py:50
  88.5 51.0 %all-to-all-start.2 = ((bf16[16,2,10,1536]{3,1,2,0:T(2,128)(2,1)}), bf16[16,2,10,1536]{3,1,2,0:T(2,128)(2,1)}, u32[]{:S(2)}, u32[]{:S(2)}) async-start(bf16[16,2,10,1536]{3,1,2,0:T(2,128)(2,1)} %copy.72), calls=%async_computation.2 | async-start | bytes 1966080 | tf_op jit(solution)/shard_map/all_to_all | solution.py:17
  96.3 207.5 %reduce-scatter.2.cloned.1.call-start = ((), (), s32[]{:S(2)}) async-start(), calls=%async_computation.8 | async-start | bytes 3981312 | tf_op jit(solution)/shard_map/reduce_scatter | solution.py:93
  97.0 58.5 %collective-permute-start = (bf16[320,1664]{1,0:T(8,128)(2,1)S(1)}, bf16[320,1664]{1,0:T(8,128)(2,1)}, u32[]{:S(2)}, u32[]{:S(2)}) collective-permute-start(bf16[320,1664]{1,0:T(8,128)(2,1)S(1)} %reshape_reshape.16), channel_id=1, source_target_pairs={{0,1},{1,0},{2,3},{3,2},{4,5},{5,4},{6,7},{7,6},{8,9},{9,8},{10,11... | collective-permute-start | bytes 3194888 | tf_op jit(solution)/shard_map/ppermute | solution.py:11
  152.1 25.0 %collective-permute-start.1 = (bf16[320,1536]{1,0:T(8,128)(2,1)}, bf16[320,1536]{1,0:T(8,128)(2,1)S(1)}, u32[]{:S(2)}, u32[]{:S(2)}) collective-permute-start(bf16[320,1536]{1,0:T(8,128)(2,1)} %reshape_reshape.18), channel_id=1, source_target_pairs={{0,1},{1,0},{2,3},{3,2},{4,5},{5,4},{6,7},{7,6},{8,9},{9,8},{10,11... | collective-permute-start | bytes 2949128 | tf_op jit(solution)/shard_map/ppermute | solution.py:11
  156.6 2.4 copy-start.2
  158.9 1.2 copy-start.4
  161.1 1.6 copy-start.7
  161.1 1.6 copy-start.9
  178.1 0.9 copy-start.10
  178.1 3.0 copy-start.12
  185.4 2.0 copy-start.3
  185.4 3.6 %copy-start.11 = (bf16[320,384]{1,0:T(8,128)(2,1)S(1)}, bf16[320,384]{1,0:T(8,128)(2,1)}, u32[]{:S(2)}) copy-start(bf16[320,384]{1,0:T(8,128)(2,1)} %copy-done.10) | copy-start | bytes 737284
  194.5 5.6 %copy-start.8 = (bf16[320,384]{1,0:T(8,128)(2,1)S(1)}, bf16[320,384]{1,0:T(8,128)(2,1)}, u32[]{:S(2)}) copy-start(bf16[320,384]{1,0:T(8,128)(2,1)} %copy-done.7) | copy-start | bytes 737284
  194.5 35.4 %collective-permute-start.2 = (bf16[320,1664]{1,0:T(8,128)(2,1)}, bf16[320,1664]{1,0:T(8,128)(2,1)}, u32[]{:S(2)}, u32[]{:S(2)}) collective-permute-start(bf16[320,1664]{1,0:T(8,128)(2,1)} %concatenate.25), channel_id=1, source_target_pairs={{0,1},{1,0},{2,3},{3,2},{4,5},{5,4},{6,7},{7,6},{8,9},{9,8},{10,11... | collective-permute-start | bytes 3194888 | tf_op jit(solution)/shard_map/ppermute | solution.py:11
  301.3 1.3 copy-start.6
  301.3 4.4 %copy-start.1 = (bf16[128,1536]{1,0:T(8,128)(2,1)S(1)}, bf16[128,1536]{1,0:T(8,128)(2,1)}, u32[]{:S(2)}) copy-start(bf16[128,1536]{1,0:T(8,128)(2,1)} %param.7) | copy-start | bytes 1179652
Sparse Core Ops, SparseCore 0:
  36.7 86.7 all-gather.1
  185.6 100.5 reduce-scatter.1
where the time goes:
time: 314 us; the launch traced here: 313 us
  waiting for transfers between devices  115 us (37%)
  blocking collectives  87.9 us (28%)
  starting transfers between devices  33.4 us (11%)
  local copies, waits for them, and re-layouts  28.4 us (9%)
  matrix products  26.3 us (8%)
  between operations  14.5 us (5%)
  other arithmetic  7.28 us (2%)
    all_to_all x2, waiting for transfers between devices, exchange(): split = lax.all_to_all(split, 'ez', split_axis=0, concat_axis=0, tiled=True)  79.3 us
    all_to_all x1, blocking collectives, exchange(): split = lax.all_to_all(split, 'ez', split_axis=0, concat_axis=0, tiled=True)  60 us
    ppermute x3, waiting for transfers between devices, swap_pair(): return lax.ppermute(value, 'rl', [(0, 1), (1, 0)])  35.5 us
    all_to_all x3, blocking collectives, exchange(): split = lax.all_to_all(split, 'ec', split_axis=1, concat_axis=1, tiled=True)  27.9 us
    all_to_all x2, starting transfers between devices, exchange(): split = lax.all_to_all(split, 'ez', split_axis=0, concat_axis=0, tiled=True)  23.6 us
    ppermute x3, starting transfers between devices, swap_pair(): return lax.ppermute(value, 'rl', [(0, 1), (1, 0)])  9.67 us
  transfers between devices with their start and end apart: 7, of which 4 were waited for; matrix products, arithmetic and copies ran while one was open for 13% of the time, Pallas kernels for 0%

commit v1 on v0

--- a/solution.py
+++ b/solution.py
@@ -15,7 +15,10 @@
     shape = blocks.shape
     split = blocks.reshape((lax.axis_size("ez"), lax.axis_size("ec")) + shape[1:])
     split = lax.all_to_all(split, "ez", split_axis=0, concat_axis=0, tiled=True)
-    split = lax.all_to_all(split, "ec", split_axis=1, concat_axis=1, tiled=True)
+    size = lax.axis_size("ec")
+    pieces = jnp.stack(jnp.split(split, size, axis=1), axis=0)
+    pieces = lax.all_to_all(pieces, "ec", split_axis=0, concat_axis=0)
+    split = jnp.concatenate(pieces, axis=1)
     return split.reshape(shape)
 
 

time: 314 us -> 314 us (level)
  waiting for transfers between devices: 115 us -> 111 us
    split x0 -> x3, local copies, waits for them, and re-layouts: none -> 4.39 us  [exchange(): pieces = jnp.stack(jnp.split(split, size, axis=1), axis=0)]
  transfers between devices with their start and end apart: 7 -> 7, of which waited for: 4 -> 4; matrix products, arithmetic and copies ran while one was open for 13% -> 14% of each run, Pallas kernels for 0% -> 0%
where the time goes in v1:
time: 314 us; the launch traced here: 311 us
  waiting for transfers between devices  111 us (35%)
  blocking collectives  88.6 us (28%)
  starting transfers between devices  33.2 us (11%)
  local copies, waits for them, and re-layouts  29.2 us (9%)
  matrix products  27.5 us (9%)
  between operations  14.5 us (5%)
  other arithmetic  7.58 us (2%)
    all_to_all x2, waiting for transfers between devices, exchange(): split = lax.all_to_all(split, 'ez', split_axis=0, concat_axis=0, tiled=True)  76.8 us
    all_to_all x1, blocking collectives, exchange(): split = lax.all_to_all(split, 'ez', split_axis=0, concat_axis=0, tiled=True)  58.3 us
    ppermute x3, waiting for transfers between devices, swap_pair(): return lax.ppermute(value, 'rl', [(0, 1), (1, 0)])  33.7 us
    all_to_all x3, blocking collectives, exchange(): pieces = lax.all_to_all(pieces, 'ec', split_axis=0, concat_axis=0)  30.3 us
    all_to_all x2, starting transfers between devices, exchange(): split = lax.all_to_all(split, 'ez', split_axis=0, concat_axis=0, tiled=True)  23.6 us
    ppermute x3, starting transfers between devices, swap_pair(): return lax.ppermute(value, 'rl', [(0, 1), (1, 0)])  9.54 us
  transfers between devices with their start and end apart: 7, of which 4 were waited for; matrix products, arithmetic and copies ran while one was open for 14% of the time, Pallas kernels for 0%

profile of v1, /device:TPU:1, one launch (start us, length us, event | category | flops | bytes accessed | tf_op | source)
XLA Modules:
  0.0 311.1 jit_solution(1079149411769462813)
XLA Ops:
  13.4 2.4 concatenate.22
  15.7 1.8 copy.106
  17.5 15.9 %all-to-all-start = ((bf16[16,2,10,1664]{3,1,2,0:T(2,128)(2,1)}), bf16[16,2,10,1664]{3,1,2,0:T(2,128)(2,1)S(1)}, u32[]{:S(2)}, u32[]{:S(2)}) async-start(bf16[16,2,10,1664]{3,1,2,0:T(2,128)(2,1)} %copy.106), calls=%async_computation | async-start | bytes 2129920 | tf_op jit(solution)/shard_map/all_to_all | solution.py:17
  37.2 2.0 copy.110
  39.2 39.9 %all-to-all-done = bf16[16,2,10,1664]{3,1,2,0:T(2,128)(2,1)S(1)} async-done(((bf16[16,2,10,1664]{3,1,2,0:T(2,128)(2,1)}), bf16[16,2,10,1664]{3,1,2,0:T(2,128)(2,1)S(1)}, u32[]{:S(2)}, u32[]{:S(2)}) %all-to-all-start) | async-done | bytes 1064992 | tf_op jit(solution)/shard_map/all_to_all | solution.py:17
  79.0 1.5 fusion.40
  80.8 10.1 %all_to_all.30 = bf16[2,16,1,10,1664]{4,1,3,2,0:T(8,128)(2,1)S(1)} all-to-all(bf16[2,16,1,10,1664]{4,1,3,2,0:T(8,128)(2,1)S(1)} %pad_maximum_fusion), channel_id=1, replica_groups=mesh['ez'=16,'ec'=2,'rh'=8,'rl'=2] {'ec'}, dimensions={0} | all-to-all | bytes 2129920 | tf_op jit(solution)/shard_map/all_to_all | solution.py:20
  90.9 7.7 %all-to-all-start.2 = ((bf16[16,2,10,1536]{3,1,2,0:T(2,128)(2,1)}), bf16[16,2,10,1536]{3,1,2,0:T(2,128)(2,1)S(1)}, u32[]{:S(2)}, u32[]{:S(2)}) async-start(bf16[16,2,10,1536]{3,1,2,0:T(2,128)(2,1)} %copy.110), calls=%async_computation.2 | async-start | bytes 1966080 | tf_op jit(solution)/shard_map/all_to_all | solution.py:17
  100.1 1.6 reshape_reshape_reshape.9
  101.8 3.1 %collective-permute-start = (bf16[320,1664]{1,0:T(8,128)(2,1)S(1)}, bf16[320,1664]{1,0:T(8,128)(2,1)}, u32[]{:S(2)}, u32[]{:S(2)}) collective-permute-start(bf16[320,1664]{1,0:T(8,128)(2,1)S(1)} %reshape_reshape_reshape.9), channel_id=1, source_target_pairs={{0,1},{1,0},{2,3},{3,2},{4,5},{5,4},{6,7},{7,6},{8,9},{9,8},{10,11... | collective-permute-start | bytes 3194888 | tf_op jit(solution)/shard_map/ppermute | solution.py:11
  104.9 36.9 %all-to-all-done.2 = bf16[16,2,10,1536]{3,1,2,0:T(2,128)(2,1)S(1)} async-done(((bf16[16,2,10,1536]{3,1,2,0:T(2,128)(2,1)}), bf16[16,2,10,1536]{3,1,2,0:T(2,128)(2,1)S(1)}, u32[]{:S(2)}, u32[]{:S(2)}) %all-to-all-start.2) | async-done | bytes 983072 | tf_op jit(solution)/shard_map/all_to_all | solution.py:17
  143.6 9.5 %all_to_all.31 = bf16[2,16,1,10,1536]{4,1,3,2,0:T(8,128)(2,1)S(1)} all-to-all(bf16[2,16,1,10,1536]{4,1,3,2,0:T(8,128)(2,1)S(1)} %pad_maximum_fusion.2), channel_id=1, replica_groups=mesh['ez'=16,'ec'=2,'rh'=8,'rl'=2] {'ec'}, dimensions={0} | all-to-all | bytes 1966080 | tf_op jit(solution)/shard_map/all_to_all | solution.py:20
  154.8 3.3 %collective-permute-start.1 = (bf16[320,1536]{1,0:T(8,128)(2,1)}, bf16[320,1536]{1,0:T(8,128)(2,1)S(1)}, u32[]{:S(2)}, u32[]{:S(2)}) collective-permute-start(bf16[320,1536]{1,0:T(8,128)(2,1)} %reshape_reshape_reshape.10), channel_id=1, source_target_pairs={{0,1},{1,0},{2,3},{3,2},{4,5},{5,4},{6,7},{7,6},{8,9},{9,8},{10,11... | collective-permute-start | bytes 2949128 | tf_op jit(solution)/shard_map/ppermute | solution.py:11
  159.3 2.1 fusion.11
  166.3 1.9 fusion.9
  168.2 1.9 fusion.6
  170.1 9.8 %collective-permute-done.1 = bf16[320,1536]{1,0:T(8,128)(2,1)S(1)} collective-permute-done((bf16[320,1536]{1,0:T(8,128)(2,1)}, bf16[320,1536]{1,0:T(8,128)(2,1)S(1)}, u32[]{:S(2)}, u32[]{:S(2)}) %collective-permute-start.1) | collective-permute-done | bytes 983072 | tf_op jit(solution)/shard_map/ppermute | solution.py:11
  181.7 2.0 convolution_bitcast_fusion.1
  183.7 2.0 convolution_bitcast_fusion.2
  185.7 2.3 fusion
  188.1 1.9 fusion.8
  190.0 2.0 fusion.2
  192.1 1.9 concatenate.25
  194.0 3.1 %collective-permute-start.2 = (bf16[320,1664]{1,0:T(8,128)(2,1)}, bf16[320,1664]{1,0:T(8,128)(2,1)}, u32[]{:S(2)}, u32[]{:S(2)}) collective-permute-start(bf16[320,1664]{1,0:T(8,128)(2,1)} %concatenate.25), channel_id=1, source_target_pairs={{0,1},{1,0},{2,3},{3,2},{4,5},{5,4},{6,7},{7,6},{8,9},{9,8},{10,11... | collective-permute-start | bytes 3194888 | tf_op jit(solution)/shard_map/ppermute | solution.py:11
  197.2 1.9 fusion.10
  199.2 2.0 fusion.1
  202.1 24.0 %collective-permute-done.2 = bf16[320,1664]{1,0:T(8,128)(2,1)} collective-permute-done((bf16[320,1664]{1,0:T(8,128)(2,1)}, bf16[320,1664]{1,0:T(8,128)(2,1)}, u32[]{:S(2)}, u32[]{:S(2)}) %collective-permute-start.2) | collective-permute-done | bytes 1064992 | tf_op jit(solution)/shard_map/ppermute | solution.py:11
  226.1 1.5 add_convert_fusion
  228.8 58.3 %all_to_all.32 = bf16[16,2,10,1664]{3,1,2,0:T(2,128)(2,1)S(1)} all-to-all(bf16[16,2,10,1664]{3,1,2,0:T(2,128)(2,1)S(1)} %copy.116), channel_id=1, replica_groups=mesh['ez'=16,'ec'=2,'rh'=8,'rl'=2] {'ez'}, dimensions={0} | all-to-all | bytes 2129920 | tf_op jit(solution)/shard_map/all_to_all | solution.py:17
  287.1 1.5 fusion.39
  288.8 10.8 %all_to_all.33 = bf16[2,16,1,10,1664]{4,1,3,2,0:T(8,128)(2,1)S(1)} all-to-all(bf16[2,16,1,10,1664]{4,1,3,2,0:T(8,128)(2,1)S(1)} %pad_maximum_fusion.1), channel_id=1, replica_groups=mesh['ez'=16,'ec'=2,'rh'=8,'rl'=2] {'ec'}, dimensions={0} | all-to-all | bytes 2129920 | tf_op jit(solution)/shard_map/all_to_all | solution.py:20
  302.3 2.0 fusion.42
  (79 shorter events, 28.3 us)
Async XLA Ops:
  7.2 4.4 %copy-start = (bf16[128,1536]{1,0:T(8,128)(2,1)S(1)}, bf16[128,1536]{1,0:T(8,128)(2,1)}, u32[]{:S(2)}) copy-start(bf16[128,1536]{1,0:T(8,128)(2,1)} %param.7) | copy-start | bytes 1179652
  17.5 15.9 %copy-start.5 = (bf16[1,48,1536]{2,1,0:T(8,128)(2,1)S(1)}, bf16[1,48,1536]{2,1,0:T(8,128)(2,1)}, u32[]{:S(2)}) copy-start(bf16[1,48,1536]{2,1,0:T(8,128)(2,1)} %param.13) | copy-start | bytes 442372
  17.5 15.9 %copy-start.6 = (bf16[1,48,1536]{2,1,0:T(8,128)(2,1)S(1)}, bf16[1,48,1536]{2,1,0:T(8,128)(2,1)}, u32[]{:S(2)}) copy-start(bf16[1,48,1536]{2,1,0:T(8,128)(2,1)} %param.12) | copy-start | bytes 442372
  17.5 16.0 %copy-start.7 = (bf16[1,48,1536]{2,1,0:T(8,128)(2,1)S(1)}, bf16[1,48,1536]{2,1,0:T(8,128)(2,1)}, u32[]{:S(2)}) copy-start(bf16[1,48,1536]{2,1,0:T(8,128)(2,1)} %param.11) | copy-start | bytes 442372
  17.5 61.5 %all-to-all-start = ((bf16[16,2,10,1664]{3,1,2,0:T(2,128)(2,1)}), bf16[16,2,10,1664]{3,1,2,0:T(2,128)(2,1)S(1)}, u32[]{:S(2)}, u32[]{:S(2)}) async-start(bf16[16,2,10,1664]{3,1,2,0:T(2,128)(2,1)} %copy.106), calls=%async_computation | async-start | bytes 2129920 | tf_op jit(solution)/shard_map/all_to_all | solution.py:17
  33.4 1.0 copy-start.4
  33.4 125.8 %all-gather.2.cloned.1.call-start = ((), (), s32[]{:S(2)}) async-start(), calls=%async_computation.7 | async-start | bytes 3981312 | tf_op jit(solution)/shard_map/all_gather | solution.py:53
  90.9 50.9 %all-to-all-start.2 = ((bf16[16,2,10,1536]{3,1,2,0:T(2,128)(2,1)}), bf16[16,2,10,1536]{3,1,2,0:T(2,128)(2,1)S(1)}, u32[]{:S(2)}, u32[]{:S(2)}) async-start(bf16[16,2,10,1536]{3,1,2,0:T(2,128)(2,1)} %copy.110), calls=%async_computation.2 | async-start | bytes 1966080 | tf_op jit(solution)/shard_map/all_to_all | solution.py:17
  98.6 203.6 %reduce-scatter.2.cloned.1.call-start = ((), (), s32[]{:S(2)}) async-start(), calls=%async_computation.8 | async-start | bytes 3981312 | tf_op jit(solution)/shard_map/reduce_scatter | solution.py:96
  101.8 56.5 %collective-permute-start = (bf16[320,1664]{1,0:T(8,128)(2,1)S(1)}, bf16[320,1664]{1,0:T(8,128)(2,1)}, u32[]{:S(2)}, u32[]{:S(2)}) collective-permute-start(bf16[320,1664]{1,0:T(8,128)(2,1)S(1)} %reshape_reshape_reshape.9), channel_id=1, source_target_pairs={{0,1},{1,0},{2,3},{3,2},{4,5},{5,4},{6,7},{7,6},{8,9},{9,8},{10,11... | collective-permute-start | bytes 3194888 | tf_op jit(solution)/shard_map/ppermute | solution.py:11
  154.8 25.0 %collective-permute-start.1 = (bf16[320,1536]{1,0:T(8,128)(2,1)}, bf16[320,1536]{1,0:T(8,128)(2,1)S(1)}, u32[]{:S(2)}, u32[]{:S(2)}) collective-permute-start(bf16[320,1536]{1,0:T(8,128)(2,1)} %reshape_reshape_reshape.10), channel_id=1, source_target_pairs={{0,1},{1,0},{2,3},{3,2},{4,5},{5,4},{6,7},{7,6},{8,9},{9,8},{10,11... | collective-permute-start | bytes 2949128 | tf_op jit(solution)/shard_map/ppermute | solution.py:11
  159.3 2.4 copy-start.2
  161.6 1.2 copy-start.3
  194.0 32.1 %collective-permute-start.2 = (bf16[320,1664]{1,0:T(8,128)(2,1)}, bf16[320,1664]{1,0:T(8,128)(2,1)}, u32[]{:S(2)}, u32[]{:S(2)}) collective-permute-start(bf16[320,1664]{1,0:T(8,128)(2,1)} %concatenate.25), channel_id=1, source_target_pairs={{0,1},{1,0},{2,3},{3,2},{4,5},{5,4},{6,7},{7,6},{8,9},{9,8},{10,11... | collective-permute-start | bytes 3194888 | tf_op jit(solution)/shard_map/ppermute | solution.py:11
  301.1 3.1 %copy-start.1 = (bf16[128,1536]{1,0:T(8,128)(2,1)S(1)}, bf16[128,1536]{1,0:T(8,128)(2,1)}, u32[]{:S(2)}) copy-start(bf16[128,1536]{1,0:T(8,128)(2,1)} %param.7) | copy-start | bytes 1179652
Sparse Core Ops, SparseCore 0:
  37.4 82.7 all-gather.1
  188.2 97.8 reduce-scatter.1
